TPU v7x, 512 devices: a whole 4x4x16 slice. The times are simulated.
512 devices in a mesh: grp: 4 (over y), seq: 32 (over z, core), mp: 4 (over x).
Axes of the slice: x: 4, y: 4, z: 16, core: 2. Of those that a mesh axis runs over, the one named last changes fastest.
Arguments:
- queries: bfloat16 [4, 4096, 2048], P('grp', 'seq', 'mp'), may hold values from -16 to 16
- d_out: bfloat16 [4, 4096, 2048], P('grp', 'seq', 'mp'), may hold values from -6 to 6
- neighbour_kv: bfloat16 [4, 256, 128, 2, 2048], P('grp', 'seq', None, None, 'mp'), may hold values from -16 to 16
- target: int32 [4, 256], P('grp', 'seq'), may hold values from -1 to 127, as said below
- bias: float32 [16, 191], P('mp'), may hold values from -6 to 6
Outputs:
- attended: bfloat16 [4, 4096, 2048], P('grp', 'seq', 'mp')
- d_query: bfloat16 [4, 4096, 2048], P('grp', 'seq', 'mp')
- d_kv: bfloat16 [4, 256, 128, 2, 2048], P('grp', 'seq', None, None, 'mp')
- d_bias: float32 [16, 191], P('mp')
Inputs may be any that keep to these rules, and one draw needn't show every extreme that they name: `target`: in each group every entry 0..127 stands in exactly one slot and -1 marks an empty slot. The slots of one index of seq hold at most 1 entries e with the same e // 4, and some index reaches that; some index of seq holds 8 entries.
All inputs are finite; a program needn't handle non-finite values.
Results may differ from a plain program's by a relative error of at most 0.011.
Values may be sent and summed in bfloat16 or wider, within the bound.
No kernel may reach another device: no remote copies, remote signals or barrier semaphores. Data moves between devices by JAX's collectives and lax.ppermute only.
A program may use at most 128 MiB of HBM per device.

v0:
```python
import jax
import jax.numpy as jnp
from jax import lax
from jax.sharding import PartitionSpec as P

STRETCH = 64
NB_LEN = 128
SEQ_LEN = 2048


def passed_along(block, axis, distance):
    devices = range(lax.axis_size(axis))
    route = [(i - distance, i) for i in devices if i - distance in devices]
    return lax.ppermute(block, axis, route)


def bias_grid(lookup, row_count, col_count):
    head_num = lookup.shape[0]
    span = row_count + col_count
    padded = jnp.pad(lookup, ((0, 0), (0, 1)))
    flattened = jnp.tile(padded, (1, row_count))
    flattened = jnp.pad(flattened, ((0, 0), (0, row_count)))
    shaped = flattened.reshape(head_num, row_count, span + 1)[:, :, :col_count]
    return shaped[:, :, ::-1]


def bias_fold(grads):
    head_num, row_count, col_count = grads.shape
    turned = grads[:, :, ::-1]
    padded = jnp.pad(turned, ((0, 0), (0, 0), (0, row_count)))
    flattened = padded.reshape(head_num, row_count * (row_count + col_count))
    flattened = flattened[:, : row_count * (row_count + col_count - 1)]
    return jnp.sum(flattened.reshape(head_num, row_count, row_count + col_count - 1), axis=1)


def take_rows(table, index, valid):
    rows = jnp.take(table, index, axis=0)
    shape = (valid.shape[0],) + (1,) * (rows.ndim - 1)
    return jnp.where(valid.reshape(shape), rows, jnp.zeros((), rows.dtype))


def exchange(block):
    return lax.all_to_all(block, "seq", split_axis=0, concat_axis=0, tiled=True)


def local(queries, d_out, neighbour_kv, target, bias):
    tok_rows = queries.shape[1]
    width_dev = queries.shape[2]
    head_count = bias.shape[0]
    head_depth = width_dev // head_count
    stretch_count = tok_rows // STRETCH
    per_owner = 2 * stretch_count
    shard_count = lax.axis_size("seq")
    my_index = lax.axis_index("seq")
    group_rows = tok_rows * shard_count
    seq_stretches = min(SEQ_LEN, group_rows) // STRETCH
    scale_factor = head_depth ** (-0.5)
    bias_rows = bias_grid(bias, STRETCH, NB_LEN).transpose(1, 0, 2)
    row_ids = jnp.arange(STRETCH)
    pair = jnp.stack([queries[0], d_out[0]], axis=1)
    pair_all = lax.all_gather(pair, "seq", axis=0, tiled=True)
    my_targets = target[0]
    slot_count = my_targets.shape[0]
    is_used = my_targets >= 0
    entry = jnp.where(is_used, my_targets, 0)
    stretch_of = entry // 2
    win_rows = stretch_of[:, None] * STRETCH + (STRETCH - 1) + row_ids[None, :]
    in_group = win_rows < group_rows
    win_rows = jnp.minimum(win_rows.reshape(-1), group_rows - 1)
    win = jnp.take(pair_all, win_rows, axis=0).reshape(slot_count, STRETCH, 2, width_dev)
    q_win = win[:, :, 0]
    g_win = win[:, :, 1]
    live_slot = (row_ids[None, :] == 0) | ((stretch_of[:, None] + 1) % seq_stretches != 0)
    q_keep = is_used[:, None] & in_group
    q_slots = jnp.where(q_keep[:, :, None], q_win, jnp.zeros((), q_win.dtype))
    g_slots = jnp.where((q_keep & live_slot)[:, :, None], g_win, jnp.zeros((), g_win.dtype))
    q_slots = q_slots.reshape(slot_count, STRETCH, head_count, head_depth)
    g_slots = g_slots.reshape(slot_count, STRETCH, head_count, head_depth)
    stored = neighbour_kv[0]
    key_rows = stored[:, :, 0].reshape(slot_count, NB_LEN, head_count, head_depth)
    value_rows = stored[:, :, 1].reshape(slot_count, NB_LEN, head_count, head_depth)
    scores = jnp.einsum("sihd,sjhd->sihj", q_slots, key_rows, preferred_element_type=jnp.float32)
    scores = scores * scale_factor + bias_rows[None]
    peak_val = jnp.max(scores, axis=-1)
    weights = jnp.exp(scores - peak_val[..., None])
    row_total = jnp.sum(weights, axis=-1)
    partial_value = jnp.einsum(
        "sihj,sjhd->sihd",
        weights.astype(jnp.bfloat16),
        value_rows,
        preferred_element_type=jnp.float32,
    )
    owner_of = jnp.where(is_used, my_targets // per_owner, -1)
    owner_match = owner_of[None, :] == jnp.arange(shard_count)[:, None]
    send_slot = jnp.argmax(owner_match, axis=1)
    send_has = jnp.any(owner_match, axis=1)
    part_send = take_rows(
        partial_value.astype(jnp.bfloat16).reshape(slot_count, STRETCH, width_dev),
        send_slot,
        send_has,
    )
    g_dot = jnp.einsum(
        "sihd,sihd->sih",
        g_slots.astype(jnp.float32),
        partial_value,
        precision=lax.Precision.HIGHEST,
    )
    mine = jnp.stack([peak_val, row_total, g_dot], axis=1)
    shared = jnp.concatenate(
        [
            mine.reshape(slot_count, -1),
            jnp.where(is_used, entry + 1, 0).astype(jnp.float32)[:, None],
        ],
        axis=1,
    )
    shared_wide = jnp.pad(shared, ((0, 0), (0, 1024 - shared.shape[1])))
    shared_all = lax.all_gather(shared_wide, "seq", tiled=True)[:, : shared.shape[1]]
    partner = entry + 1 - 2 * (entry % 2)
    partner_at = jnp.argmax(
        shared_all[None, :, -1] == (partner + 1).astype(jnp.float32)[:, None], axis=1
    )
    theirs = jnp.take(shared_all[:, :-1], partner_at, axis=0).reshape(mine.shape)
    both_peak = jnp.maximum(mine[:, 0], theirs[:, 0])
    mine_f = jnp.exp(mine[:, 0] - both_peak)
    theirs_f = jnp.exp(theirs[:, 0] - both_peak)
    both_total = mine_f * mine[:, 1] + theirs_f * theirs[:, 1]
    lse_slots = both_peak + jnp.log(both_total)
    dd_slots = (mine_f * mine[:, 2] + theirs_f * theirs[:, 2]) / both_total
    dd_slots = jnp.where(is_used[:, None, None], dd_slots, 0.0)
    part_recv = exchange(part_send)
    own_entries = my_index * per_owner + jnp.arange(per_owner)
    own_at = jnp.argmax(
        shared_all[None, :, -1] == (own_entries + 1).astype(jnp.float32)[:, None], axis=1
    )
    held_by = own_at // slot_count
    parts_own = jnp.take(part_recv, held_by, axis=0).astype(jnp.float32)
    parts_own = parts_own.reshape(stretch_count, 2, STRETCH, head_count, head_depth)
    stats_own = jnp.take(shared_all[:, :-1], own_at, axis=0).reshape(
        stretch_count, 2, 3, STRETCH, head_count
    )
    peaks_own = stats_own[:, :, 0]
    totals_own = stats_own[:, :, 1]
    stretch_ids = my_index * stretch_count + jnp.arange(stretch_count)
    is_live = (row_ids[None, :] == 0) | ((stretch_ids[:, None] + 1) % seq_stretches != 0)
    live_rows = is_live.astype(jnp.float32)
    top_peak = jnp.max(peaks_own, axis=1)
    factor = jnp.exp(peaks_own - top_peak[:, None])
    denominator = jnp.sum(factor * totals_own, axis=1)
    combined = jnp.sum(factor[..., None] * parts_own, axis=1) / denominator[..., None]
    combined = combined * live_rows[:, :, None, None]
    att_win = combined.astype(jnp.bfloat16).reshape(tok_rows, width_dev)
    att_before = passed_along(att_win[tok_rows - STRETCH :], "seq", 1)
    prob_full = jnp.exp(scores - lse_slots[..., None])
    prob_low = prob_full.astype(jnp.bfloat16)
    grad_prob = jnp.einsum(
        "sihd,sjhd->sihj", g_slots, value_rows, preferred_element_type=jnp.float32
    )
    grad_scores = prob_full * (grad_prob - dd_slots[..., None])
    scores_low = grad_scores.astype(jnp.bfloat16)
    grad_rows = (
        jnp.einsum("sihj,sjhd->sihd", scores_low, key_rows, preferred_element_type=jnp.float32)
        * scale_factor
    )
    mix_probs = jnp.stack([scores_low, prob_low], axis=1)
    mix_rows = jnp.stack([q_slots, g_slots], axis=1)
    grad_kv = jnp.einsum(
        "sxihj,sxihd->sjxhd", mix_probs, mix_rows, preferred_element_type=jnp.float32
    )
    kv_scale = jnp.array([scale_factor, 1.0], jnp.float32)[None, None, :, None, None]
    d_kv = (grad_kv * kv_scale).astype(jnp.bfloat16).reshape(slot_count, NB_LEN, 2, width_dev)
    bias_part = bias_fold(jnp.sum(grad_scores, axis=0).transpose(1, 0, 2))
    dq_rows = jnp.zeros((shard_count, stretch_count, STRETCH, width_dev), jnp.bfloat16)
    dq_owner = jnp.where(is_used, owner_of, shard_count)
    dq_rows = dq_rows.at[dq_owner, stretch_of % stretch_count].set(
        grad_rows.astype(jnp.bfloat16).reshape(slot_count, STRETCH, width_dev), mode="drop"
    )
    grad_win = lax.psum_scatter(dq_rows, "seq", scatter_dimension=0, tiled=True)
    grad_win = grad_win.reshape(tok_rows, width_dev)
    grad_before = passed_along(grad_win[tok_rows - STRETCH :], "seq", 1)
    attended = jnp.concatenate([att_before[1:], att_win[: tok_rows - STRETCH + 1]])
    d_query = jnp.concatenate([grad_before[1:], grad_win[: tok_rows - STRETCH + 1]])
    raw_sum = lax.psum(lax.psum(bias_part, "seq"), "grp")
    squares = lax.psum(jnp.sum(raw_sum * raw_sum), "mp")
    d_bias = raw_sum * jnp.minimum(1.0, 1.0 / jnp.sqrt(squares + 1e-12))
    return (attended[None], d_query[None], d_kv[None], d_bias)


def solution(mesh):
    in_specs = (
        P("grp", "seq", "mp"),
        P("grp", "seq", "mp"),
        P("grp", "seq", None, None, "mp"),
        P("grp", "seq"),
        P("mp", None),
    )
    out_specs = (
        P("grp", "seq", "mp"),
        P("grp", "seq", "mp"),
        P("grp", "seq", None, None, "mp"),
        P("mp", None),
    )
    return jax.shard_map(local, mesh=mesh, in_specs=in_specs, out_specs=out_specs, check_vma=False)
```

profile of v0, /device:TPU:1, one launch (start us, length us, event | category | flops | bytes accessed | tf_op | source)
XLA Modules:
  0.0 341.9 jit_solution(12824938684409181369)
XLA Ops:
  12.3 3.8 %copy.106 = bf16[1,8,128,2,512]{2,4,1,3,0:T(8,128)(2,1)} copy(bf16[1,8,128,2,512]{4,3,2,1,0:T(2,128)(2,1)S(1)} %copy-done.8) | data formatting | bytes 4194304 | tf_op args[2]
  16.9 2.8 fusion.54
  19.7 75.7 %all-gather.3.cloned.1.call-done = bf16[4096,2,512]{2,1,0:T(2,128)(2,1)} async-done(((bf16[128,2,512]{2,1,0:T(2,128)(2,1)}), bf16[4096,2,512]{2,1,0:T(2,128)(2,1)}) %all-gather.3.cloned.1.call-update) | async-done | bytes 8388624 | tf_op jit(solution)/shard_map/all_gather | solution.py:61
  95.4 6.4 %gather_fusion = bf16[512,2,512]{2,1,0:T(2,128)(2,1)S(1)} fusion(bf16[4096,2,512]{2,1,0:T(2,128)(2,1)} %all-gather.3.cloned.1.call-done, s32[1024]{0:T(1024)S(1)} %pad_clamp_fusion.4), kind=kCustom, calls=%fused_computation | custom fusion | bytes 2099200 | tf_op jit(solution)/shard_map/jit(_take)/gather | solution.py:70
  105.1 2.0 multiply_reduce_fusion
  110.1 2.0 gather_fusion.2
  112.1 3.3 select_select_fusion
  115.3 7.8 %all-to-all-start = ((bf16[32,64,512]{2,1,0:T(8,128)(2,1)}), bf16[32,64,512]{2,1,0:T(8,128)(2,1)}, u32[]{:S(2)}, u32[]{:S(2)}) async-start(bf16[32,64,512]{2,1,0:T(8,128)(2,1)} %select_select_fusion), calls=%async_computation | async-start | bytes 4194304 | tf_op jit(solution)/shard_map/all_to_all | solution.py:43
  123.2 76.4 %all-gather.5.cloned.1.call-done = f32[256,1024]{1,0:T(8,128)} async-done(((f32[8,1024]{1,0:T(8,128)}), f32[256,1024]{1,0:T(8,128)}) %all-gather.5.cloned.1.call-update) | async-done | bytes 1048592 | tf_op jit(solution)/shard_map/all_gather | solution.py:117
  201.9 2.1 slice.108
  203.9 2.3 gather_fusion.4
  212.4 2.4 broadcast_in_dim.169
  214.9 2.5 scatter_fusion
  222.0 45.5 %psum.21 = f32[4,191]{1,0:T(4,128)S(1)} all-reduce(f32[4,191]{1,0:T(4,128)S(1)} %reduce_sum.58), channel_id=1, replica_groups=mesh['grp'=4,'seq'=32,'mp'=4] {'seq'}, use_global_device_ids=true, to_apply=%region_13.14 | all-reduce | flops 764 | bytes 6112 | tf_op jit(solution)/shard_map/psum | solution.py:182
  267.5 8.4 %psum.22 = f32[4,191]{1,0:T(4,128)S(1)} all-reduce(f32[4,191]{1,0:T(4,128)S(1)} %psum.21), channel_id=1, replica_groups=mesh['grp'=4,'seq'=32,'mp'=4] {'grp'}, use_global_device_ids=true, to_apply=%region_14.15 | all-reduce | flops 764 | bytes 6112 | tf_op jit(solution)/shard_map/psum | solution.py:182
  277.7 10.2 %psum.23 = f32[]{:T(128)} all-reduce(f32[]{:T(128)} %multiply_reduce_fusion.2), channel_id=1, replica_groups=mesh['grp'=4,'seq'=32,'mp'=4] {'mp'}, use_global_device_ids=true, to_apply=%region_16.17 | all-reduce | flops 1 | bytes 8 | tf_op jit(solution)/shard_map/psum | solution.py:183
  289.9 1.7 gather_fusion.1
  293.0 2.2 multiply_convert_fusion
  295.2 3.8 %copy.129 = bf16[1,8,128,2,512]{4,3,2,1,0:T(2,128)(2,1)} copy(bf16[1,8,128,2,512]{2,4,3,1,0:T(8,128)(2,1)S(1)} %bitcast.165) | data formatting | bytes 4194304
  299.8 2.2 gather_fusion.3
  302.9 5.1 %collective-permute-start = (bf16[64,512]{1,0:T(8,128)(2,1)S(1)}, bf16[64,512]{1,0:T(8,128)(2,1)S(1)}, u32[]{:S(2)}, u32[]{:S(2)}) collective-permute-start(bf16[64,512]{1,0:T(8,128)(2,1)S(1)} %bitcast.180), channel_id=1, source_target_pairs={{0,4},{4,8},{8,12},{12,16},{16,20},{20,24},{24,28},{28,32},{32,36}... | collective-permute-start | bytes 196616 | tf_op jit(solution)/shard_map/ppermute | solution.py:14
  308.2 1.9 collective-permute-done
  310.1 18.2 %reduce-scatter.2.cloned.1.call-done = bf16[1,2,64,512]{3,2,1,0:T(8,128)(2,1)} async-done(((bf16[32,2,64,512]{3,2,1,0:T(8,128)(2,1)}), bf16[1,2,64,512]{3,2,1,0:T(8,128)(2,1)}) %reduce-scatter.2.cloned.1.call-update) | async-done | bytes 131088 | tf_op jit(solution)/shard_map/reduce_scatter | solution.py:177
  329.1 3.4 collective-permute-start.1
  (157 shorter events, 34.7 us)
Async XLA Ops:
  7.2 5.2 %copy-start.8 = (bf16[1,8,128,2,512]{4,3,2,1,0:T(2,128)(2,1)S(1)}, bf16[1,8,128,2,512]{4,3,2,1,0:T(2,128)(2,1)}, u32[]{:S(2)}) copy-start(bf16[1,8,128,2,512]{4,3,2,1,0:T(2,128)(2,1)} %param.8) | copy-start | bytes 6291460
  7.2 88.3 %all-gather.3.cloned.1.call-start = ((), (), s32[]{:S(2)}) async-start(), calls=%async_computation.2 | async-start | bytes 8650752 | tf_op jit(solution)/shard_map/all_gather | solution.py:61
  9.4 190.3 %all-gather.5.cloned.1.call-start = ((), (), s32[]{:S(2)}) async-start(), calls=%async_computation.3 | async-start | bytes 1081344 | tf_op jit(solution)/shard_map/all_gather | solution.py:117
  10.1 6.1 %copy-start.21 = (pred[8]{0:T(512)(128)(4,1)}, pred[8]{0:T(512)(128)(4,1)S(1)}, u32[]{:S(2)}) copy-start(pred[8]{0:T(512)(128)(4,1)S(1)} %get-tuple-element.54) | copy-start | bytes 28
  16.1 3.6 %copy-start.23 = (pred[64]{0:T(512)(128)(4,1)}, pred[64]{0:T(512)(128)(4,1)S(1)}, u32[]{:S(2)}) copy-start(pred[64]{0:T(512)(128)(4,1)S(1)} %iota_compare_fusion.2) | copy-start | bytes 196
  16.2 86.1 %copy-start.17 = (pred[8,64]{1,0:T(8,128)(4,1)}, pred[8,64]{1,0:T(8,128)(4,1)S(1)}, u32[]{:S(2)}) copy-start(pred[8,64]{1,0:T(8,128)(4,1)S(1)} %get-tuple-element.51) | copy-start | bytes 1540
  16.2 86.9 %copy-start.15 = (pred[8,64]{1,0:T(8,128)(4,1)}, pred[8,64]{1,0:T(8,128)(4,1)S(1)}, u32[]{:S(2)}) copy-start(pred[8,64]{1,0:T(8,128)(4,1)S(1)} %get-tuple-element.50) | copy-start | bytes 1540
  105.1 3.1 copy-start.22
  115.3 184.5 %all-to-all-start = ((bf16[32,64,512]{2,1,0:T(8,128)(2,1)}), bf16[32,64,512]{2,1,0:T(8,128)(2,1)}, u32[]{:S(2)}, u32[]{:S(2)}) async-start(bf16[32,64,512]{2,1,0:T(8,128)(2,1)} %select_select_fusion), calls=%async_computation | async-start | bytes 4194304 | tf_op jit(solution)/shard_map/all_to_all | solution.py:43
  123.2 86.5 %copy-start.9 = (bf16[8,64,4,128]{3,2,1,0:T(4,128)(2,1)S(1)}, bf16[8,64,4,128]{3,2,1,0:T(4,128)(2,1)}, u32[]{:S(2)}) copy-start(bf16[8,64,4,128]{3,2,1,0:T(4,128)(2,1)} %get-tuple-element.35) | copy-start | bytes 1572868
  123.2 205.1 %reduce-scatter.2.cloned.1.call-start = ((), (), s32[]{:S(2)}) async-start(), calls=%async_computation.4 | async-start | bytes 4325376 | tf_op jit(solution)/shard_map/reduce_scatter | solution.py:177
  200.6 3.3 copy-start.19
  207.9 3.5 %copy-start.3 = (bf16[8,128,1,512]{1,3,0,2:T(8,128)(2,1)S(1)}, bf16[8,128,1,512]{1,3,0,2:T(8,128)(2,1)}, u32[]{:S(2)}) copy-start(bf16[8,128,1,512]{1,3,0,2:T(8,128)(2,1)} %get-tuple-element.38) | copy-start | bytes 3145732
  217.4 3.0 copy-start.1
  219.3 57.2 %copy-start.6 = (bf16[8,1,64,4,128]{4,3,2,0,1:T(4,128)(2,1)S(1)}, bf16[8,1,64,4,128]{4,3,2,0,1:T(4,128)(2,1)}, u32[]{:S(2)}) copy-start(bf16[8,1,64,4,128]{4,3,2,0,1:T(4,128)(2,1)} %squeeze.45) | copy-start | bytes 1572868
  219.3 57.2 %copy-start.16 = (pred[8,64]{1,0:T(8,128)(4,1)S(1)}, pred[8,64]{1,0:T(8,128)(4,1)}, u32[]{:S(2)}) copy-start(pred[8,64]{1,0:T(8,128)(4,1)} %copy-done.15) | copy-start | bytes 1540
  219.3 57.2 %copy-start.18 = (pred[8,64]{1,0:T(8,128)(4,1)S(1)}, pred[8,64]{1,0:T(8,128)(4,1)}, u32[]{:S(2)}) copy-start(pred[8,64]{1,0:T(8,128)(4,1)} %copy-done.17) | copy-start | bytes 1540
  220.3 56.2 %copy-start.7 = (bf16[8,1,64,4,128]{4,3,2,0,1:T(4,128)(2,1)S(1)}, bf16[8,1,64,4,128]{4,3,2,0,1:T(4,128)(2,1)}, u32[]{:S(2)}) copy-start(bf16[8,1,64,4,128]{4,3,2,0,1:T(4,128)(2,1)} %squeeze.44) | copy-start | bytes 1572868
  221.3 66.6 %copy-start.20 = (f32[256]{0:T(256)S(1)}, f32[256]{0:T(256)}, u32[]{:S(2)}) copy-start(f32[256]{0:T(256)} %copy-done.19) | copy-start | bytes 3076
  221.4 71.2 %copy-start.11 = (f32[8,64,4]{1,2,0:T(4,128)S(1)}, f32[8,64,4]{1,2,0:T(4,128)}, u32[]{:S(2)}) copy-start(f32[8,64,4]{1,2,0:T(4,128)} %copy-done.10) | copy-start | bytes 24580
  295.2 3.8 %copy-start.26 = (pred[2,2]{1,0:T(4,128)(4,1)S(1)}, pred[2,2]{1,0:T(4,128)(4,1)}, u32[]{:S(2)}) copy-start(pred[2,2]{1,0:T(4,128)(4,1)} %broadcast_in_dim.155) | copy-start | bytes 16
  299.0 3.0 copy-start.25
  302.9 7.1 %collective-permute-start = (bf16[64,512]{1,0:T(8,128)(2,1)S(1)}, bf16[64,512]{1,0:T(8,128)(2,1)S(1)}, u32[]{:S(2)}, u32[]{:S(2)}) collective-permute-start(bf16[64,512]{1,0:T(8,128)(2,1)S(1)} %bitcast.180), channel_id=1, source_target_pairs={{0,4},{4,8},{8,12},{12,16},{16,20},{20,24},{24,28},{28,32},{32,36}... | collective-permute-start | bytes 196616 | tf_op jit(solution)/shard_map/ppermute | solution.py:14
  329.1 5.5 %collective-permute-start.1 = (bf16[64,512]{1,0:T(8,128)(2,1)S(1)}, bf16[64,512]{1,0:T(8,128)(2,1)S(1)}, u32[]{:S(2)}, u32[]{:S(2)}) collective-permute-start(bf16[64,512]{1,0:T(8,128)(2,1)S(1)} %slice_bitcast_fusion.1), channel_id=1, source_target_pairs={{0,4},{4,8},{8,12},{12,16},{16,20},{20,24},{24,28},{28,32},{32,36}... | collective-permute-start | bytes 196616 | tf_op jit(solution)/shard_map/ppermute | solution.py:14
  (9 other events, 16.0 us)
Sparse Core Ops, SparseCore 0:
  10.1 85.2 all-gather.2
  108.3 91.2 all-gather.4
  217.5 110.7 reduce-scatter.1
where the time goes:
time: 343 us; the launch traced here: 342 us
  waiting for transfers between devices  173 us (50%)
  blocking collectives  64.2 us (19%)
  local copies, waits for them, and re-layouts  47.5 us (14%)
  other arithmetic  19.6 us (6%)
  starting transfers between devices  16.5 us (5%)
  between operations  15 us (4%)
  matrix products  6.32 us (2%)
    all_gather x1, waiting for transfers between devices, local(): lax.all_gather(shared_wide, 'seq', tiled=True)[:, :shared.shape[1]]  76.4 us
    all_gather x1, waiting for transfers between devices, local(): pair_all = lax.all_gather(pair, 'seq', axis=0, tiled=True)  75.7 us
    psum x2, blocking collectives, local(): raw_sum = lax.psum(lax.psum(bias_part, 'seq'), 'grp')  53.9 us
    reduce_scatter x1, waiting for transfers between devices, local(): grad_win = lax.psum_scatter(dq_rows, 'seq', scatter_dimension=0, tiled=True)  18.2 us
    psum x1, blocking collectives, local(): squares = lax.psum(jnp.sum(raw_sum * raw_sum), 'mp')  10.2 us
    unnamed x58, local copies, waits for them, and re-layouts  9.33 us
    ppermute x2, starting transfers between devices, passed_along(): return lax.ppermute(block, axis, route)  8.55 us
    all_to_all x1, starting transfers between devices, exchange(): return lax.all_to_all(block, 'seq', split_axis=0, concat_axis=0, tiled=True)  7.84 us
  transfers between devices with their start and end apart: 6, of which 5 were waited for; matrix products, arithmetic and copies ran while one was open for 16% of the time, Pallas kernels for 0%

commit v1 on v0

--- a/solution.py
+++ b/solution.py
@@ -179,7 +179,7 @@
     grad_before = passed_along(grad_win[tok_rows - STRETCH :], "seq", 1)
     attended = jnp.concatenate([att_before[1:], att_win[: tok_rows - STRETCH + 1]])
     d_query = jnp.concatenate([grad_before[1:], grad_win[: tok_rows - STRETCH + 1]])
-    raw_sum = lax.psum(lax.psum(bias_part, "seq"), "grp")
+    raw_sum = jnp.sum(lax.all_gather(lax.psum(bias_part, "seq"), "grp"), axis=0)
     squares = lax.psum(jnp.sum(raw_sum * raw_sum), "mp")
     d_bias = raw_sum * jnp.minimum(1.0, 1.0 / jnp.sqrt(squares + 1e-12))
     return (attended[None], d_query[None], d_kv[None], d_bias)

time: 343 us -> 342 us (level)
    all_gather x0 -> x1, blocking collectives: none -> 9.6 us  [local(): raw_sum = jnp.sum(lax.all_gather(lax.psum(bias_part, 'seq'), 'grp'), axis=0)]
    psum x2 -> x1, blocking collectives: 53.9 us -> 46.7 us  [local(): raw_sum = jnp.sum(lax.all_gather(lax.psum(bias_part, 'seq'), 'grp'), axis=0)]
    unnamed x58 -> x62, local copies, waits for them, and re-layouts: 9.33 us -> 9.33 us
where the time goes in v1:
time: 342 us; the launch traced here: 341 us
  waiting for transfers between devices  171 us (50%)
  blocking collectives  63.9 us (19%)
  local copies, waits for them, and re-layouts  47.5 us (14%)
  other arithmetic  19.7 us (6%)
  starting transfers between devices  17.9 us (5%)
  between operations  15 us (4%)
  matrix products  6 us (2%)
    all_gather x1, waiting for transfers between devices, local(): lax.all_gather(shared_wide, 'seq', tiled=True)[:, :shared.shape[1]]  78.4 us
    all_gather x1, waiting for transfers between devices, local(): pair_all = lax.all_gather(pair, 'seq', axis=0, tiled=True)  75.7 us
    psum x1, blocking collectives, local(): raw_sum = jnp.sum(lax.all_gather(lax.psum(bias_part, 'seq'), 'grp'), axis=0)  46.7 us
    reduce_scatter x1, waiting for transfers between devices, local(): grad_win = lax.psum_scatter(dq_rows, 'seq', scatter_dimension=0, tiled=True)  14.9 us
    ppermute x2, starting transfers between devices, passed_along(): return lax.ppermute(block, axis, route)  9.98 us
    all_gather x1, blocking collectives, local(): raw_sum = jnp.sum(lax.all_gather(lax.psum(bias_part, 'seq'), 'grp'), axis=0)  9.6 us
    unnamed x62, local copies, waits for them, and re-layouts  9.33 us
    all_to_all x1, starting transfers between devices, exchange(): return lax.all_to_all(block, 'seq', split_axis=0, concat_axis=0, tiled=True)  7.84 us
  transfers between devices with their start and end apart: 6, of which 5 were waited for; matrix products, arithmetic and copies ran while one was open for 16% of the time, Pallas kernels for 0%

profile of v1, /device:TPU:1, one launch (start us, length us, event | category | flops | bytes accessed | tf_op | source)
XLA Modules:
  0.0 341.4 jit_solution(5611892943813630152)
XLA Ops:
  12.3 3.8 %copy.106 = bf16[1,8,128,2,512]{2,4,1,3,0:T(8,128)(2,1)} copy(bf16[1,8,128,2,512]{4,3,2,1,0:T(2,128)(2,1)S(1)} %copy-done.8) | data formatting | bytes 4194304 | tf_op args[2]
  16.9 2.8 fusion.54
  19.7 75.7 %all-gather.3.cloned.1.call-done = bf16[4096,2,512]{2,1,0:T(2,128)(2,1)} async-done(((bf16[128,2,512]{2,1,0:T(2,128)(2,1)}), bf16[4096,2,512]{2,1,0:T(2,128)(2,1)}) %all-gather.3.cloned.1.call-update) | async-done | bytes 8388624 | tf_op jit(solution)/shard_map/all_gather | solution.py:61
  95.4 6.4 %gather_fusion = bf16[512,2,512]{2,1,0:T(2,128)(2,1)S(1)} fusion(bf16[4096,2,512]{2,1,0:T(2,128)(2,1)} %all-gather.3.cloned.1.call-done, s32[1024]{0:T(1024)S(1)} %pad_clamp_fusion.4), kind=kCustom, calls=%fused_computation | custom fusion | bytes 2099200 | tf_op jit(solution)/shard_map/jit(_take)/gather | solution.py:70
  105.1 2.0 multiply_reduce_fusion
  110.1 2.0 gather_fusion.2
  112.1 3.3 select_select_fusion
  115.3 7.8 %all-to-all-start = ((bf16[32,64,512]{2,1,0:T(8,128)(2,1)}), bf16[32,64,512]{2,1,0:T(8,128)(2,1)}, u32[]{:S(2)}, u32[]{:S(2)}) async-start(bf16[32,64,512]{2,1,0:T(8,128)(2,1)} %select_select_fusion), calls=%async_computation | async-start | bytes 4194304 | tf_op jit(solution)/shard_map/all_to_all | solution.py:43
  123.3 78.4 %all-gather.5.cloned.1.call-done = f32[256,1024]{1,0:T(8,128)} async-done(((f32[8,1024]{1,0:T(8,128)}), f32[256,1024]{1,0:T(8,128)}) %all-gather.5.cloned.1.call-update) | async-done | bytes 1048592 | tf_op jit(solution)/shard_map/all_gather | solution.py:117
  203.9 2.1 slice.108
  206.0 2.3 gather_fusion.4
  214.4 2.4 broadcast_in_dim.169
  216.9 2.5 scatter_fusion
  224.0 46.7 %psum.14 = f32[1,4,191]{2,1,0:T(4,128)S(1)} all-reduce(f32[1,4,191]{2,1,0:T(4,128)S(1)} %bitcast.182), channel_id=1, replica_groups=mesh['grp'=4,'seq'=32,'mp'=4] {'seq'}, use_global_device_ids=true, to_apply=%region_13.14 | all-reduce | flops 764 | bytes 6112 | tf_op jit(solution)/shard_map/psum | solution.py:182
  270.7 9.6 %all_gather.15 = f32[4,4,191]{2,1,0:T(4,128)S(1)} all-gather(f32[1,4,191]{2,1,0:T(4,128)S(1)} %psum.14), channel_id=1, replica_groups=mesh['grp'=4,'seq'=32,'mp'=4] {'grp'}, dimensions={0}, use_global_device_ids=true | all-gather | bytes 15280 | tf_op jit(solution)/shard_map/all_gather | solution.py:182
  282.1 7.6 %psum.15 = f32[]{:T(128)} all-reduce(f32[]{:T(128)} %multiply_reduce_fusion.2), channel_id=1, replica_groups=mesh['grp'=4,'seq'=32,'mp'=4] {'mp'}, use_global_device_ids=true, to_apply=%region_16.17 | all-reduce | flops 1 | bytes 8 | tf_op jit(solution)/shard_map/psum | solution.py:183
  291.6 1.7 gather_fusion.1
  294.8 1.9 multiply_convert_fusion
  296.7 3.8 %copy.129 = bf16[1,8,128,2,512]{4,3,2,1,0:T(2,128)(2,1)} copy(bf16[1,8,128,2,512]{2,4,3,1,0:T(8,128)(2,1)S(1)} %bitcast.166) | data formatting | bytes 4194304
  301.3 2.2 gather_fusion.3
  304.4 6.6 %collective-permute-start = (bf16[64,512]{1,0:T(8,128)(2,1)S(1)}, bf16[64,512]{1,0:T(8,128)(2,1)S(1)}, u32[]{:S(2)}, u32[]{:S(2)}) collective-permute-start(bf16[64,512]{1,0:T(8,128)(2,1)S(1)} %bitcast.181), channel_id=1, source_target_pairs={{0,4},{4,8},{8,12},{12,16},{16,20},{20,24},{24,28},{28,32},{32,36}... | collective-permute-start | bytes 196616 | tf_op jit(solution)/shard_map/ppermute | solution.py:14
  311.2 1.8 collective-permute-done
  313.0 14.9 %reduce-scatter.2.cloned.1.call-done = bf16[1,2,64,512]{3,2,1,0:T(8,128)(2,1)} async-done(((bf16[32,2,64,512]{3,2,1,0:T(8,128)(2,1)}), bf16[1,2,64,512]{3,2,1,0:T(8,128)(2,1)}) %reduce-scatter.2.cloned.1.call-update) | async-done | bytes 131088 | tf_op jit(solution)/shard_map/reduce_scatter | solution.py:177
  328.7 3.3 collective-permute-start.1
  (162 shorter events, 34.7 us)
Async XLA Ops:
  7.2 5.2 %copy-start.8 = (bf16[1,8,128,2,512]{4,3,2,1,0:T(2,128)(2,1)S(1)}, bf16[1,8,128,2,512]{4,3,2,1,0:T(2,128)(2,1)}, u32[]{:S(2)}) copy-start(bf16[1,8,128,2,512]{4,3,2,1,0:T(2,128)(2,1)} %param.8) | copy-start | bytes 6291460
  7.2 88.3 %all-gather.3.cloned.1.call-start = ((), (), s32[]{:S(2)}) async-start(), calls=%async_computation.2 | async-start | bytes 8650752 | tf_op jit(solution)/shard_map/all_gather | solution.py:61
  9.4 192.3 %all-gather.5.cloned.1.call-start = ((), (), s32[]{:S(2)}) async-start(), calls=%async_computation.3 | async-start | bytes 1081344 | tf_op jit(solution)/shard_map/all_gather | solution.py:117
  10.1 6.1 %copy-start.23 = (pred[8]{0:T(512)(128)(4,1)}, pred[8]{0:T(512)(128)(4,1)S(1)}, u32[]{:S(2)}) copy-start(pred[8]{0:T(512)(128)(4,1)S(1)} %get-tuple-element.54) | copy-start | bytes 28
  16.1 3.6 %copy-start.25 = (pred[64]{0:T(512)(128)(4,1)}, pred[64]{0:T(512)(128)(4,1)S(1)}, u32[]{:S(2)}) copy-start(pred[64]{0:T(512)(128)(4,1)S(1)} %iota_compare_fusion.2) | copy-start | bytes 196
  16.2 86.1 %copy-start.19 = (pred[8,64]{1,0:T(8,128)(4,1)}, pred[8,64]{1,0:T(8,128)(4,1)S(1)}, u32[]{:S(2)}) copy-start(pred[8,64]{1,0:T(8,128)(4,1)S(1)} %get-tuple-element.51) | copy-start | bytes 1540
  16.2 86.9 %copy-start.17 = (pred[8,64]{1,0:T(8,128)(4,1)}, pred[8,64]{1,0:T(8,128)(4,1)S(1)}, u32[]{:S(2)}) copy-start(pred[8,64]{1,0:T(8,128)(4,1)S(1)} %get-tuple-element.50) | copy-start | bytes 1540
  105.1 3.1 copy-start.24
  115.3 186.0 %all-to-all-start = ((bf16[32,64,512]{2,1,0:T(8,128)(2,1)}), bf16[32,64,512]{2,1,0:T(8,128)(2,1)}, u32[]{:S(2)}, u32[]{:S(2)}) async-start(bf16[32,64,512]{2,1,0:T(8,128)(2,1)} %select_select_fusion), calls=%async_computation | async-start | bytes 4194304 | tf_op jit(solution)/shard_map/all_to_all | solution.py:43
  123.2 88.6 %copy-start.9 = (bf16[8,64,4,128]{3,2,1,0:T(4,128)(2,1)S(1)}, bf16[8,64,4,128]{3,2,1,0:T(4,128)(2,1)}, u32[]{:S(2)}) copy-start(bf16[8,64,4,128]{3,2,1,0:T(4,128)(2,1)} %get-tuple-element.35) | copy-start | bytes 1572868
  123.2 204.7 %reduce-scatter.2.cloned.1.call-start = ((), (), s32[]{:S(2)}) async-start(), calls=%async_computation.4 | async-start | bytes 4325376 | tf_op jit(solution)/shard_map/reduce_scatter | solution.py:177
  202.7 3.3 copy-start.21
  210.0 3.5 %copy-start.3 = (bf16[8,128,1,512]{1,3,0,2:T(8,128)(2,1)S(1)}, bf16[8,128,1,512]{1,3,0,2:T(8,128)(2,1)}, u32[]{:S(2)}) copy-start(bf16[8,128,1,512]{1,3,0,2:T(8,128)(2,1)} %get-tuple-element.38) | copy-start | bytes 3145732
  221.4 59.5 %copy-start.6 = (bf16[8,1,64,4,128]{4,3,2,0,1:T(4,128)(2,1)S(1)}, bf16[8,1,64,4,128]{4,3,2,0,1:T(4,128)(2,1)}, u32[]{:S(2)}) copy-start(bf16[8,1,64,4,128]{4,3,2,0,1:T(4,128)(2,1)} %squeeze.45) | copy-start | bytes 1572868
  221.4 59.5 %copy-start.18 = (pred[8,64]{1,0:T(8,128)(4,1)S(1)}, pred[8,64]{1,0:T(8,128)(4,1)}, u32[]{:S(2)}) copy-start(pred[8,64]{1,0:T(8,128)(4,1)} %copy-done.17) | copy-start | bytes 1540
  221.4 59.5 %copy-start.20 = (pred[8,64]{1,0:T(8,128)(4,1)S(1)}, pred[8,64]{1,0:T(8,128)(4,1)}, u32[]{:S(2)}) copy-start(pred[8,64]{1,0:T(8,128)(4,1)} %copy-done.19) | copy-start | bytes 1540
  222.4 58.5 %copy-start.7 = (bf16[8,1,64,4,128]{4,3,2,0,1:T(4,128)(2,1)S(1)}, bf16[8,1,64,4,128]{4,3,2,0,1:T(4,128)(2,1)}, u32[]{:S(2)}) copy-start(bf16[8,1,64,4,128]{4,3,2,0,1:T(4,128)(2,1)} %squeeze.44) | copy-start | bytes 1572868
  223.4 66.4 %copy-start.22 = (f32[256]{0:T(256)S(1)}, f32[256]{0:T(256)}, u32[]{:S(2)}) copy-start(f32[256]{0:T(256)} %copy-done.21) | copy-start | bytes 3076
  223.5 71.0 %copy-start.13 = (f32[8,64,4]{1,2,0:T(4,128)S(1)}, f32[8,64,4]{1,2,0:T(4,128)}, u32[]{:S(2)}) copy-start(f32[8,64,4]{1,2,0:T(4,128)} %copy-done.12) | copy-start | bytes 24580
  282.1 12.7 %copy-start.10 = (bf16[8,1,64,4,128]{4,2,3,1,0:T(8,128)(2,1)S(1)}, bf16[8,1,64,4,128]{4,2,3,1,0:T(8,128)(2,1)}, u32[]{:S(2)}) copy-start(bf16[8,1,64,4,128]{4,2,3,1,0:T(8,128)(2,1)} %get-tuple-element.57) | copy-start | bytes 1572868
  282.1 12.7 %copy-start.11 = (bf16[8,1,64,4,128]{4,2,3,1,0:T(8,128)(2,1)S(1)}, bf16[8,1,64,4,128]{4,2,3,1,0:T(8,128)(2,1)}, u32[]{:S(2)}) copy-start(bf16[8,1,64,4,128]{4,2,3,1,0:T(8,128)(2,1)} %get-tuple-element.58) | copy-start | bytes 1572868
  296.7 3.8 %copy-start.28 = (pred[2,2]{1,0:T(4,128)(4,1)S(1)}, pred[2,2]{1,0:T(4,128)(4,1)}, u32[]{:S(2)}) copy-start(pred[2,2]{1,0:T(4,128)(4,1)} %broadcast_in_dim.155) | copy-start | bytes 16
  304.4 8.6 %collective-permute-start = (bf16[64,512]{1,0:T(8,128)(2,1)S(1)}, bf16[64,512]{1,0:T(8,128)(2,1)S(1)}, u32[]{:S(2)}, u32[]{:S(2)}) collective-permute-start(bf16[64,512]{1,0:T(8,128)(2,1)S(1)} %bitcast.181), channel_id=1, source_target_pairs={{0,4},{4,8},{8,12},{12,16},{16,20},{20,24},{24,28},{28,32},{32,36}... | collective-permute-start | bytes 196616 | tf_op jit(solution)/shard_map/ppermute | solution.py:14
  328.7 5.4 %collective-permute-start.1 = (bf16[64,512]{1,0:T(8,128)(2,1)S(1)}, bf16[64,512]{1,0:T(8,128)(2,1)S(1)}, u32[]{:S(2)}, u32[]{:S(2)}) collective-permute-start(bf16[64,512]{1,0:T(8,128)(2,1)S(1)} %slice_bitcast_fusion.1), channel_id=1, source_target_pairs={{0,4},{4,8},{8,12},{12,16},{16,20},{20,24},{24,28},{28,32},{32,36}... | collective-permute-start | bytes 196616 | tf_op jit(solution)/shard_map/ppermute | solution.py:14
  (11 other events, 22.0 us)
Sparse Core Ops, SparseCore 0:
  10.1 85.2 all-gather.2
  108.3 93.3 all-gather.4
  219.5 108.3 reduce-scatter.1
